TPU v7x, 256 devices: a whole 4x4x8 slice. The times are simulated.
256 devices in a mesh: user: 16 (over z, core), item: 16 (over y, x).
Axes of the slice: x: 4, y: 4, z: 8, core: 2. Of those that a mesh axis runs over, the one named last changes fastest.
Arguments:
- ratings: bfloat16 [30720, 128, 128], P(('user', 'item')), may hold values from -6 to 6
- weights: bfloat16 [30720, 128, 128], P(('user', 'item')), may hold values from 0.19921875 to 2
- row_masks: int32 [30720, 4], P(('user', 'item')), may hold values from -2147483648 to 2147483646
- tile_users: int32 [30720], P(('user', 'item')), may hold values from 0 to 15
- tile_items: int32 [30720], P(('user', 'item')), may hold values from 0 to 15
- tile_counts: int32 [256], P(('user', 'item')), may hold values from 1 to 120
- users: float32 [32768, 128], P(('user', 'item')), may hold values from -1.8 to 1.8
- items: float32 [2048, 128], P('item'), may hold values from -1.8 to 1.8
Outputs:
- new_users: float32 [32768, 128], P(('user', 'item'))
- new_items: float32 [2048, 128], P('item')
All inputs are finite; a program needn't handle non-finite values.
Results may differ from a plain program's by a relative error of at most 0.002.
Values may be sent and summed in bfloat16 or wider, within the bound.
No kernel may reach another device: no remote copies, remote signals or barrier semaphores. Data moves between devices by JAX's collectives and lax.ppermute only.
A program may use at most 64 MiB of HBM per device.

v0:
```python
import jax
import jax.numpy as jnp
from jax import lax
from jax.sharding import PartitionSpec as P

STEPS = 2
STEP_SCALE = 4.0
DECAY_RATE = 0.02


def unpack_rows(packed, side):
    lanes = jnp.arange(side, dtype=jnp.int32)
    picked = packed[:, lanes // 32]
    return jnp.bitwise_and(jnp.right_shift(picked, lanes % 32), 1)


def tile_terms(user_panel, item_panel, tile_vals, tile_wts, packed, user_ids, item_ids, live_mask):
    side = tile_vals.shape[1]
    rowbits = unpack_rows(packed, side).astype(jnp.float32) * live_mask[:, None]
    weighted = tile_wts.astype(jnp.float32) * rowbits[:, :, None]
    user_rows = jnp.take(user_panel, user_ids, axis=0)
    item_rows = jnp.take(item_panel, item_ids, axis=0)
    predicted = jnp.einsum("tbr,tcr->tbc", user_rows, item_rows, preferred_element_type=jnp.float32)
    residual = (weighted * (tile_vals.astype(jnp.float32) - predicted)).astype(jnp.bfloat16)
    user_part = jnp.einsum("tbc,tcr->tbr", residual, item_rows, preferred_element_type=jnp.float32)
    item_part = jnp.einsum("tbc,tbr->tcr", residual, user_rows, preferred_element_type=jnp.float32)
    return (user_part, item_part, jnp.sum(weighted, axis=2), jnp.sum(weighted, axis=1))


def sweep(user_panel, item_panel, tiles, live_count, totals):
    per_block = 8
    blocks = (live_count + per_block - 1) // per_block

    def one_block(block, state):
        anchor = block * per_block

        def cut_block(array):
            return lax.dynamic_slice_in_dim(array, anchor, per_block, 0)

        tile_vals, tile_wts, packed, user_ids, item_ids = [cut_block(array) for array in tiles]
        slot_index = anchor + jnp.arange(per_block, dtype=jnp.int32)
        live_mask = (slot_index < live_count).astype(jnp.float32)
        user_part, item_part, user_rowsum, item_rowsum = tile_terms(
            user_panel, item_panel, tile_vals, tile_wts, packed, user_ids, item_ids, live_mask
        )
        user_sum, user_diag, item_sum, item_diag = state
        return (
            user_sum.at[user_ids].add(user_part),
            user_diag.at[user_ids].add(user_rowsum),
            item_sum.at[item_ids].add(item_part),
            item_diag.at[item_ids].add(item_rowsum),
        )

    return lax.fori_loop(0, blocks, one_block, totals)


def on_device(ratings, weights, row_masks, tile_users, tile_items, tile_counts, users, items):
    side = ratings.shape[1]
    rank = users.shape[1]
    count_here = tile_counts[0]
    own_tiles = (ratings, weights, row_masks, tile_users, tile_items)
    for iteration in range(STEPS):
        user_panel, item_panel = (
            lax.all_gather(users.astype(jnp.bfloat16), "item", axis=0, tiled=True),
            lax.all_gather(items.astype(jnp.bfloat16), "item", axis=0, tiled=True),
        )
        user_panel = user_panel.reshape(-1, side, rank)
        item_panel = item_panel.reshape(-1, side, rank)
        user_count = user_panel.shape[0]
        item_count = item_panel.shape[0]
        totals = (
            jnp.zeros((user_count, side, rank), jnp.float32),
            jnp.zeros((user_count, side), jnp.float32),
            jnp.zeros((item_count, side, rank), jnp.float32),
            jnp.zeros((item_count, side), jnp.float32),
        )
        user_sum, user_diag, item_sum, item_diag = sweep(
            user_panel, item_panel, own_tiles, count_here, totals
        )
        user_grad = user_sum.reshape(-1, rank)
        user_diag = user_diag.reshape(-1)
        item_grad = item_sum.reshape(-1, rank)
        item_diag = item_diag.reshape(-1)
        user_grad, user_diag, item_grad, item_diag = (
            lax.psum_scatter(user_grad, "item", scatter_dimension=0, tiled=True),
            lax.psum_scatter(user_diag, "item", scatter_dimension=0, tiled=True),
            lax.psum_scatter(item_grad, "item", scatter_dimension=0, tiled=True),
            lax.psum_scatter(item_diag, "item", scatter_dimension=0, tiled=True),
        )
        item_grad, item_diag = lax.psum((item_grad, item_diag), "user")
        user_weight = 2.0 * side + user_diag
        item_weight = 2.0 * side + item_diag
        users = users + STEP_SCALE * (user_grad / user_weight[:, None] - DECAY_RATE * users)
        items = items + STEP_SCALE * (item_grad / item_weight[:, None] - DECAY_RATE * items)
    return (users, items)


def solution(mesh):
    return jax.shard_map(
        on_device,
        mesh=mesh,
        in_specs=(
            P(("user", "item"), None, None),
            P(("user", "item"), None, None),
            P(("user", "item"), None),
            P(("user", "item")),
            P(("user", "item")),
            P(("user", "item")),
            P(("user", "item"), None),
            P("item", None),
        ),
        out_specs=(P(("user", "item"), None), P("item", None)),
        check_vma=False,
    )
```

profile of v0, /device:TPU:1, one launch (start us, length us, event | category | flops | bytes accessed | tf_op | source)
XLA Modules:
  0.0 1030.7 jit_solution(3896531610678982321)
XLA Ops:
  9.6 21.8 %all_gather.13 = bf16[2048,128]{1,0:T(8,128)(2,1)} all-gather(bf16[128,128]{1,0:T(8,128)(2,1)S(1)} %convert_element_type.89), channel_id=1, replica_groups=mesh['user'=16,'item'=16] {'item'}, dimensions={0}, use_global_device_ids=true | all-gather | bytes 557056 | tf_op jit(solution)/shard_map/all_gather | solution.py:65
  31.3 19.9 %all_gather.12 = bf16[2048,128]{1,0:T(8,128)(2,1)} all-gather(bf16[128,128]{1,0:T(8,128)(2,1)S(1)} %convert_element_type.88), channel_id=1, replica_groups=mesh['user'=16,'item'=16] {'item'}, dimensions={0}, use_global_device_ids=true | all-gather | bytes 557056 | tf_op jit(solution)/shard_map/all_gather | solution.py:64
  51.5 41.9 %while.36 = (s32[]{:T(128)}, f32[16,128,128]{2,1,0:T(8,128)S(1)}, f32[16,128]{1,0:T(8,128)S(1)}, f32[16,128,128]{2,1,0:T(8,128)S(1)}, f32[16,128]{1,0:T(8,128)S(...) while((s32[]{:T(128)}, f32[16,128,128]{2,1,0:T(8,128)S(1)}, ...), condition=%wide.region_7.9_spmd, body=%wide.region_0.8_spmd.sunk | while | flops 102769920 | bytes 7946063 | solution.py:54
  57.2 1.6 gather_fusion.2
  58.9 1.6 gather_fusion.1
  60.5 1.4 fusion.43
  71.2 1.6 gather_fusion.2
  72.8 1.6 gather_fusion.1
  74.5 1.4 fusion.43
  85.1 1.6 gather_fusion.2
  86.8 1.6 gather_fusion.1
  97.2 175.6 %all-reduce.5 = (f32[2048]{0:T(1024)S(1)}, f32[2048]{0:T(1024)S(1)}) all-reduce(f32[2048]{0:T(1024)S(1)} %bitcast.50, f32[2048]{0:T(1024)S(1)} %bitcast.49), channel_id=3, replica_groups=mesh['user'=16,'item'=16] {'item'}, use_global_device_ids=true, to_apply=%region_9.11.clone | all-reduce | flops 4096 | bytes 32768
  272.9 96.4 %psum.29 = f32[128]{0:T(128)S(1)} all-reduce(f32[128]{0:T(128)S(1)} %dynamic-slice.3), channel_id=1, replica_groups=mesh['user'=16,'item'=16] {'user'}, use_global_device_ids=true, to_apply=%region_13.15 | all-reduce | flops 128 | bytes 1024 | tf_op jit(solution)/shard_map/psum | solution.py:90
  369.5 58.9 %reduce-scatter.5.cloned.1.call-done = f32[128,128]{1,0:T(8,128)} async-done(((f32[2048,128]{1,0:T(8,128)}), f32[128,128]{1,0:T(8,128)}) %reduce-scatter.5.cloned.1.call-update) | async-done | bytes 65552 | tf_op jit(solution)/shard_map/reduce_scatter | solution.py:85
  429.4 19.8 %all_gather.14 = bf16[2048,128]{1,0:T(8,128)(2,1)} all-gather(bf16[128,128]{1,0:T(8,128)(2,1)S(1)} %fusion.20), channel_id=1, replica_groups=mesh['user'=16,'item'=16] {'item'}, dimensions={0}, use_global_device_ids=true | all-gather | bytes 557056 | tf_op jit(solution)/shard_map/all_gather | solution.py:64
  449.2 82.0 %all-reduce.9.cloned.1.call-done = f32[128,128]{1,0:T(8,128)} async-done(((f32[128,128]{1,0:T(8,128)}), f32[128,128]{1,0:T(8,128)}) %all-reduce.9.cloned.1.call-update) | async-done | bytes 65552 | tf_op jit(solution)/shard_map/psum | solution.py:90
  532.1 21.0 %all_gather.15 = bf16[2048,128]{1,0:T(8,128)(2,1)} all-gather(bf16[128,128]{1,0:T(8,128)(2,1)S(1)} %fusion.21), channel_id=1, replica_groups=mesh['user'=16,'item'=16] {'item'}, dimensions={0}, use_global_device_ids=true | all-gather | bytes 557056 | tf_op jit(solution)/shard_map/all_gather | solution.py:65
  553.3 41.9 %while.37 = (s32[]{:T(128)}, f32[16,128,128]{2,1,0:T(8,128)S(1)}, f32[16,128]{1,0:T(8,128)S(1)}, f32[16,128,128]{2,1,0:T(8,128)S(1)}, f32[16,128]{1,0:T(8,128)S(...) while((s32[]{:T(128)}, f32[16,128,128]{2,1,0:T(8,128)S(1)}, ...), condition=%wide.region_21.23_spmd, body=%wide.region_14.22_spmd.sunk | while | flops 102769920 | bytes 7946063 | solution.py:54
  559.0 1.6 gather_fusion.5
  560.6 1.6 gather_fusion.4
  562.3 1.4 fusion.50
  572.9 1.6 gather_fusion.5
  574.6 1.6 gather_fusion.4
  586.9 1.6 gather_fusion.5
  588.6 1.6 gather_fusion.4
  590.2 1.4 fusion.50
  597.0 177.4 %all-reduce.4 = (f32[2048]{0:T(1024)S(1)}, f32[2048]{0:T(1024)S(1)}) all-reduce(f32[2048]{0:T(1024)S(1)} %bitcast.48, f32[2048]{0:T(1024)S(1)} %bitcast.47), channel_id=7, replica_groups=mesh['user'=16,'item'=16] {'item'}, use_global_device_ids=true, to_apply=%region_23.25.clone | all-reduce | flops 4096 | bytes 32768
  774.4 87.9 %psum.31 = f32[128]{0:T(128)S(1)} all-reduce(f32[128]{0:T(128)S(1)} %dynamic-slice.7), channel_id=1, replica_groups=mesh['user'=16,'item'=16] {'user'}, use_global_device_ids=true, to_apply=%region_27.29 | all-reduce | flops 128 | bytes 1024 | tf_op jit(solution)/shard_map/psum | solution.py:90
  862.4 57.2 %reduce-scatter.9.cloned.1.call-done = f32[128,128]{1,0:T(8,128)} async-done(((f32[2048,128]{1,0:T(8,128)}), f32[128,128]{1,0:T(8,128)}) %reduce-scatter.9.cloned.1.call-update) | async-done | bytes 65552 | tf_op jit(solution)/shard_map/reduce_scatter | solution.py:85
  919.6 1.6 multiply_add_fusion.1
  921.3 101.0 %all-reduce.11.cloned.1.call-done = f32[128,128]{1,0:T(8,128)} async-done(((f32[128,128]{1,0:T(8,128)}), f32[128,128]{1,0:T(8,128)}) %all-reduce.11.cloned.1.call-update) | async-done | bytes 65552 | tf_op jit(solution)/shard_map/psum | solution.py:90
  1022.3 1.6 multiply_add_fusion
  (195 shorter events, 66.6 us)
Async XLA Ops:
  7.2 362.3 %reduce-scatter.7.cloned.1.call-start = ((), (), s32[]{:S(2)}) async-start(), calls=%async_computation.5 | async-start | bytes 1114112 | tf_op jit(solution)/shard_map/reduce_scatter | solution.py:87
  51.5 377.0 %copy-start.4 = (f32[128,128]{1,0:T(8,128)S(1)}, f32[128,128]{1,0:T(8,128)}, u32[]{:S(2)}) copy-start(f32[128,128]{1,0:T(8,128)} %param.20) | copy-start | bytes 196612
  51.5 479.7 %copy-start.5 = (f32[128,128]{1,0:T(8,128)S(1)}, f32[128,128]{1,0:T(8,128)}, u32[]{:S(2)}) copy-start(f32[128,128]{1,0:T(8,128)} %param.21) | copy-start | bytes 196612
  53.8 8.2 copy-start.6
  53.8 8.2 copy-start.8
  53.8 8.2 copy-start.10
  67.7 8.2 copy-start.6
  67.7 8.2 copy-start.8
  67.7 8.2 copy-start.10
  81.7 8.2 copy-start.6
  81.7 8.2 copy-start.8
  81.7 8.2 copy-start.10
  93.4 1.0 copy-start.2
  93.4 1.4 copy-start.3
  94.5 334.0 %reduce-scatter.5.cloned.1.call-start = ((), (), s32[]{:S(2)}) async-start(), calls=%async_computation.4 | async-start | bytes 1114112 | tf_op jit(solution)/shard_map/reduce_scatter | solution.py:85
  95.2 435.9 %all-reduce.9.cloned.1.call-start = ((), (), s32[]{:S(2)}) async-start(), calls=%async_computation.6 | async-start | bytes 131072 | tf_op jit(solution)/shard_map/psum | solution.py:90
  369.4 183.7 %copy-start.13 = (f32[128]{0:T(128)}, f32[128]{0:T(128)S(1)}, u32[]{:S(2)}) copy-start(f32[128]{0:T(128)S(1)} %dynamic-slice_add_fusion.1) | copy-start | bytes 1540
  369.4 183.7 %copy-start.12 = (f32[128]{0:T(128)}, f32[128]{0:T(128)S(1)}, u32[]{:S(2)}) copy-start(f32[128]{0:T(128)S(1)} %broadcast_add_fusion.1) | copy-start | bytes 1540
  369.5 492.9 %reduce-scatter.11.cloned.1.call-start = ((), (), s32[]{:S(2)}) async-start(), calls=%async_computation.8 | async-start | bytes 1114112 | tf_op jit(solution)/shard_map/reduce_scatter | solution.py:87
  555.5 8.2 copy-start.7
  555.5 8.2 copy-start.9
  555.5 8.2 copy-start.11
  569.5 8.2 copy-start.7
  569.5 8.2 copy-start.9
  569.5 8.2 copy-start.11
  583.5 8.2 copy-start.7
  583.5 8.2 copy-start.9
  583.5 8.2 copy-start.11
  595.3 1.0 copy-start
  595.3 1.4 copy-start.1
  596.3 323.3 %reduce-scatter.9.cloned.1.call-start = ((), (), s32[]{:S(2)}) async-start(), calls=%async_computation.7 | async-start | bytes 1114112 | tf_op jit(solution)/shard_map/reduce_scatter | solution.py:85
  596.9 425.4 %all-reduce.11.cloned.1.call-start = ((), (), s32[]{:S(2)}) async-start(), calls=%async_computation.9 | async-start | bytes 131072 | tf_op jit(solution)/shard_map/psum | solution.py:90
Sparse Core Ops, SparseCore 0:
  94.6 252.5 reduce-scatter.6
  351.1 77.3 reduce-scatter.4
  430.8 100.3 all-reduce.8
  596.4 242.5 reduce-scatter.10
  842.4 77.2 reduce-scatter.8
  921.9 100.2 all-reduce.10
where the time goes:
time: 1040 us; the launch traced here: 1030 us
  blocking collectives  620 us (60%)
  waiting for transfers between devices  300 us (29%)
  other arithmetic  45.4 us (4%)
  local copies, waits for them, and re-layouts  32.9 us (3%)
  matrix products  15.8 us (2%)
  between operations  15.6 us (2%)
    unnamed x2, blocking collectives  353 us
    psum x2, blocking collectives, on_device(): item_grad, item_diag = lax.psum((item_grad, item_diag), 'user')  184 us
    psum x2, waiting for transfers between devices, on_device(): item_grad, item_diag = lax.psum((item_grad, item_diag), 'user')  183 us
    reduce_scatter x2, waiting for transfers between devices, on_device(): lax.psum_scatter(user_grad, 'item', scatter_dimension=0, tiled=True)  116 us
    all_gather x2, blocking collectives, on_device(): lax.all_gather(items.astype(jnp.bfloat16), 'item', axis=0, tiled=True)  42.7 us
    all_gather x2, blocking collectives, on_device(): lax.all_gather(users.astype(jnp.bfloat16), 'item', axis=0, tiled=True)  39.7 us
  transfers between devices with their start and end apart: 6, of which 4 were waited for; matrix products, arithmetic and copies ran while one was open for 0% of the time, Pallas kernels for 0%

commit v1 on v0

--- a/solution.py
+++ b/solution.py
@@ -6,6 +6,13 @@
 STEPS = 2
 STEP_SCALE = 4.0
 DECAY_RATE = 0.02
+
+
+def all_by_exchange(x, mesh_axis, dim):
+    size = lax.axis_size(mesh_axis)
+    blocks = jnp.stack([x for _ in range(size)])
+    blocks = lax.all_to_all(blocks, mesh_axis, split_axis=0, concat_axis=0)
+    return jnp.concatenate(blocks, axis=dim)
 
 
 def unpack_rows(packed, side):
@@ -61,7 +68,7 @@
     own_tiles = (ratings, weights, row_masks, tile_users, tile_items)
     for iteration in range(STEPS):
         user_panel, item_panel = (
-            lax.all_gather(users.astype(jnp.bfloat16), "item", axis=0, tiled=True),
+            all_by_exchange(users.astype(jnp.bfloat16), "item", 0),
             lax.all_gather(items.astype(jnp.bfloat16), "item", axis=0, tiled=True),
         )
         user_panel = user_panel.reshape(-1, side, rank)

time: 1040 us -> 1010 us (0.971)
  blocking collectives: 620 us -> 564 us
  waiting for transfers between devices: 300 us -> 318 us
  starting transfers between devices: 0.24 us -> 12.1 us
    reduce_scatter x2, waiting for transfers between devices: 116 us -> 57.3 us  [on_device(): lax.psum_scatter(user_grad, 'item', scatter_dimension=0, tiled=True)]
    reduce_scatter x2, waiting for transfers between devices: 0.01 us -> 56.3 us  [on_device(): lax.psum_scatter(item_grad, 'item', scatter_dimension=0, tiled=True)]
    all_gather x2 -> x0, blocking collectives: 39.7 us -> none  [on_device(): lax.all_gather(users.astype(jnp.bfloat16), 'item', axis=0, tiled=True)]
    psum x2, waiting for transfers between devices: 183 us -> 204 us  [on_device(): item_grad, item_diag = lax.psum((item_grad, item_diag), 'user')]
    all_to_all x0 -> x2, starting transfers between devices: none -> 11.9 us  [all_by_exchange(): blocks = lax.all_to_all(blocks, mesh_axis, split_axis=0, concat_axis=0)]
  transfers between devices with their start and end apart: 6 -> 8, of which waited for: 4 -> 4; matrix products, arithmetic and copies ran while one was open for 0% -> 1% of each run, Pallas kernels for 0% -> 0%
where the time goes in v1:
time: 1010 us; the launch traced here: 1000 us
  blocking collectives  564 us (56%)
  waiting for transfers between devices  318 us (31%)
  other arithmetic  44.6 us (4%)
  local copies, waits for them, and re-layouts  34.7 us (3%)
  between operations  15.6 us (2%)
  matrix products  14 us (1%)
  starting transfers between devices  12.1 us (1%)
    unnamed x2, blocking collectives  345 us
    psum x2, waiting for transfers between devices, on_device(): item_grad, item_diag = lax.psum((item_grad, item_diag), 'user')  204 us
    psum x2, blocking collectives, on_device(): item_grad, item_diag = lax.psum((item_grad, item_diag), 'user')  175 us
    reduce_scatter x2, waiting for transfers between devices, on_device(): lax.psum_scatter(user_grad, 'item', scatter_dimension=0, tiled=True)  57.3 us
    reduce_scatter x2, waiting for transfers between devices, on_device(): lax.psum_scatter(item_grad, 'item', scatter_dimension=0, tiled=True)  56.3 us
    all_gather x2, blocking collectives, on_device(): lax.all_gather(items.astype(jnp.bfloat16), 'item', axis=0, tiled=True)  44 us
  transfers between devices with their start and end apart: 8, of which 4 were waited for; matrix products, arithmetic and copies ran while one was open for 1% of the time, Pallas kernels for 0%

profile of v1, /device:TPU:1, one launch (start us, length us, event | category | flops | bytes accessed | tf_op | source)
XLA Modules:
  0.0 1003.6 jit_solution(14753085723311536902)
XLA Ops:
  8.9 7.6 all-to-all-start
  18.1 23.0 %all_gather.6 = bf16[2048,128]{1,0:T(8,128)(2,1)} all-gather(bf16[128,128]{1,0:T(8,128)(2,1)S(1)} %convert_element_type.89), channel_id=1, replica_groups=mesh['user'=16,'item'=16] {'item'}, dimensions={0}, use_global_device_ids=true | all-gather | bytes 557056 | tf_op jit(solution)/shard_map/all_gather | solution.py:72
  41.4 39.1 %while.36 = (s32[]{:T(128)}, f32[16,128,128]{2,1,0:T(8,128)S(1)}, f32[16,128]{1,0:T(8,128)S(1)}, f32[16,128,128]{2,1,0:T(8,128)S(1)}, f32[16,128]{1,0:T(8,128)S(...) while((s32[]{:T(128)}, f32[16,128,128]{2,1,0:T(8,128)S(1)}, ...), condition=%wide.region_7.9_spmd, body=%wide.region_0.8_spmd.sunk | while | flops 102769920 | bytes 7945691 | solution.py:61
  47.0 1.6 gather_fusion.2
  48.7 1.6 gather_fusion.1
  50.3 1.4 fusion.43
  60.0 1.6 gather_fusion.2
  61.7 1.6 gather_fusion.1
  73.0 1.6 gather_fusion.2
  74.7 1.6 gather_fusion.1
  84.2 167.7 %all-reduce.5 = (f32[2048]{0:T(1024)S(1)}, f32[2048]{0:T(1024)S(1)}) all-reduce(f32[2048]{0:T(1024)S(1)} %bitcast.48, f32[2048]{0:T(1024)S(1)} %bitcast.47), channel_id=3, replica_groups=mesh['user'=16,'item'=16] {'item'}, use_global_device_ids=true, to_apply=%region_9.11.clone | all-reduce | flops 4096 | bytes 32768
  252.0 86.9 %psum.29 = f32[128]{0:T(128)S(1)} all-reduce(f32[128]{0:T(128)S(1)} %dynamic-slice.3), channel_id=1, replica_groups=mesh['user'=16,'item'=16] {'user'}, use_global_device_ids=true, to_apply=%region_13.15 | all-reduce | flops 128 | bytes 1024 | tf_op jit(solution)/shard_map/psum | solution.py:97
  340.8 4.2 all-to-all-start.1
  345.1 56.3 %reduce-scatter.7.cloned.1.call-done = f32[128,128]{1,0:T(8,128)} async-done(((f32[2048,128]{1,0:T(8,128)}), f32[128,128]{1,0:T(8,128)}) %reduce-scatter.7.cloned.1.call-update) | async-done | bytes 65552 | tf_op jit(solution)/shard_map/reduce_scatter | solution.py:94
  401.5 102.5 %all-reduce.9.cloned.1.call-done = f32[128,128]{1,0:T(8,128)} async-done(((f32[128,128]{1,0:T(8,128)}), f32[128,128]{1,0:T(8,128)}) %all-reduce.9.cloned.1.call-update) | async-done | bytes 65552 | tf_op jit(solution)/shard_map/psum | solution.py:97
  505.0 21.0 %all_gather.7 = bf16[2048,128]{1,0:T(8,128)(2,1)} all-gather(bf16[128,128]{1,0:T(8,128)(2,1)S(1)} %fusion.21), channel_id=1, replica_groups=mesh['user'=16,'item'=16] {'item'}, dimensions={0}, use_global_device_ids=true | all-gather | bytes 557056 | tf_op jit(solution)/shard_map/all_gather | solution.py:72
  526.2 41.9 %while.37 = (s32[]{:T(128)}, f32[16,128,128]{2,1,0:T(8,128)S(1)}, f32[16,128]{1,0:T(8,128)S(1)}, f32[16,128,128]{2,1,0:T(8,128)S(1)}, f32[16,128]{1,0:T(8,128)S(...) while((s32[]{:T(128)}, f32[16,128,128]{2,1,0:T(8,128)S(1)}, ...), condition=%wide.region_21.23_spmd, body=%wide.region_14.22_spmd.sunk | while | flops 102769920 | bytes 7946063 | solution.py:61
  531.9 1.6 gather_fusion.5
  533.5 1.6 gather_fusion.4
  535.2 1.4 fusion.50
  545.8 1.6 gather_fusion.5
  547.5 1.6 gather_fusion.4
  549.1 1.4 fusion.50
  559.8 1.6 gather_fusion.5
  561.5 1.6 gather_fusion.4
  563.1 1.4 fusion.50
  569.8 177.4 %all-reduce.4 = (f32[2048]{0:T(1024)S(1)}, f32[2048]{0:T(1024)S(1)}) all-reduce(f32[2048]{0:T(1024)S(1)} %bitcast.46, f32[2048]{0:T(1024)S(1)} %bitcast.45), channel_id=7, replica_groups=mesh['user'=16,'item'=16] {'item'}, use_global_device_ids=true, to_apply=%region_23.25.clone | all-reduce | flops 4096 | bytes 32768
  747.3 87.8 %psum.31 = f32[128]{0:T(128)S(1)} all-reduce(f32[128]{0:T(128)S(1)} %dynamic-slice.7), channel_id=1, replica_groups=mesh['user'=16,'item'=16] {'user'}, use_global_device_ids=true, to_apply=%region_27.29 | all-reduce | flops 128 | bytes 1024 | tf_op jit(solution)/shard_map/psum | solution.py:97
  835.3 57.3 %reduce-scatter.9.cloned.1.call-done = f32[128,128]{1,0:T(8,128)} async-done(((f32[2048,128]{1,0:T(8,128)}), f32[128,128]{1,0:T(8,128)}) %reduce-scatter.9.cloned.1.call-update) | async-done | bytes 65552 | tf_op jit(solution)/shard_map/reduce_scatter | solution.py:92
  892.5 1.6 multiply_add_fusion.1
  894.1 101.0 %all-reduce.11.cloned.1.call-done = f32[128,128]{1,0:T(8,128)} async-done(((f32[128,128]{1,0:T(8,128)}), f32[128,128]{1,0:T(8,128)}) %all-reduce.11.cloned.1.call-update) | async-done | bytes 65552 | tf_op jit(solution)/shard_map/psum | solution.py:97
  995.1 1.6 multiply_add_fusion
  (181 shorter events, 65.8 us)
Async XLA Ops:
  8.9 32.2 %all-to-all-start = ((bf16[16,128,128]{2,1,0:T(8,128)(2,1)}), bf16[16,128,128]{2,1,0:T(8,128)(2,1)}, u32[]{:S(2)}, u32[]{:S(2)}) async-start(bf16[16,128,128]{2,1,0:T(8,128)(2,1)} %stack.4), calls=%async_computation | async-start | bytes 1048576 | tf_op jit(solution)/shard_map/all_to_all | solution.py:14
  16.6 322.4 %reduce-scatter.5.cloned.1.call-start = ((), (), s32[]{:S(2)}) async-start(), calls=%async_computation.6 | async-start | bytes 1114112 | tf_op jit(solution)/shard_map/reduce_scatter | solution.py:92
  41.4 297.6 %copy-start.4 = (f32[128,128]{1,0:T(8,128)S(1)}, f32[128,128]{1,0:T(8,128)}, u32[]{:S(2)}) copy-start(f32[128,128]{1,0:T(8,128)} %param.20) | copy-start | bytes 196612
  80.5 1.0 copy-start.3
  80.5 1.4 copy-start.2
  80.5 423.6 %copy-start.5 = (f32[128,128]{1,0:T(8,128)S(1)}, f32[128,128]{1,0:T(8,128)}, u32[]{:S(2)}) copy-start(f32[128,128]{1,0:T(8,128)} %param.21) | copy-start | bytes 196612
  81.5 319.9 %reduce-scatter.7.cloned.1.call-start = ((), (), s32[]{:S(2)}) async-start(), calls=%async_computation.7 | async-start | bytes 1114112 | tf_op jit(solution)/shard_map/reduce_scatter | solution.py:94
  338.9 187.0 %copy-start.9 = (f32[128]{0:T(128)}, f32[128]{0:T(128)S(1)}, u32[]{:S(2)}) copy-start(f32[128]{0:T(128)S(1)} %dynamic-slice_add_fusion.1) | copy-start | bytes 1540
  340.8 185.2 %all-to-all-start.1 = ((bf16[16,128,128]{2,1,0:T(8,128)(2,1)}), bf16[16,128,128]{2,1,0:T(8,128)(2,1)}, u32[]{:S(2)}, u32[]{:S(2)}) async-start(bf16[16,128,128]{2,1,0:T(8,128)(2,1)} %stack.5), calls=%async_computation.2 | async-start | bytes 1048576 | tf_op jit(solution)/shard_map/all_to_all | solution.py:14
  345.0 159.0 %all-reduce.9.cloned.1.call-start = ((), (), s32[]{:S(2)}) async-start(), calls=%async_computation.8 | async-start | bytes 131072 | tf_op jit(solution)/shard_map/psum | solution.py:97
  401.4 433.8 %reduce-scatter.11.cloned.1.call-start = ((), (), s32[]{:S(2)}) async-start(), calls=%async_computation.10 | async-start | bytes 1114112 | tf_op jit(solution)/shard_map/reduce_scatter | solution.py:94
  401.5 124.5 %copy-start.10 = (f32[128]{0:T(128)}, f32[128]{0:T(128)S(1)}, u32[]{:S(2)}) copy-start(f32[128]{0:T(128)S(1)} %broadcast_add_fusion.1) | copy-start | bytes 1540
  528.4 8.2 copy-start.6
  528.4 8.2 copy-start.7
  528.4 8.2 copy-start.8
  542.4 8.2 copy-start.6
  542.4 8.2 copy-start.7
  542.4 8.2 copy-start.8
  556.4 8.2 copy-start.6
  556.4 8.2 copy-start.7
  556.4 8.2 copy-start.8
  568.1 1.0 copy-start
  568.1 1.4 copy-start.1
  569.2 323.3 %reduce-scatter.9.cloned.1.call-start = ((), (), s32[]{:S(2)}) async-start(), calls=%async_computation.9 | async-start | bytes 1114112 | tf_op jit(solution)/shard_map/reduce_scatter | solution.py:92
  569.8 425.3 %all-reduce.11.cloned.1.call-start = ((), (), s32[]{:S(2)}) async-start(), calls=%async_computation.11 | async-start | bytes 131072 | tf_op jit(solution)/shard_map/psum | solution.py:97
Sparse Core Ops, SparseCore 0:
  81.6 235.6 reduce-scatter.4
  321.3 80.0 reduce-scatter.6
  403.7 100.2 all-reduce.8
  569.3 242.5 reduce-scatter.10
  815.2 77.2 reduce-scatter.8
  894.8 100.2 all-reduce.10
